TPU v7x, 512 devices: a whole 4x4x16 slice. The times are simulated.
512 devices in a mesh: dp: 32 (over x, y, core), expert: 16 (over z).
Axes of the slice: x: 4, y: 4, z: 16, core: 2. Of those that a mesh axis runs over, the one named last changes fastest.
Arguments:
- tokens: bfloat16 [4096, 2048], P('dp', 'expert'), may hold values from -6 to 6
- route_weight: bfloat16 [4096, 8], P('dp'), may hold values from 0.049804688 to 0.44921875
- expert_ids: int32 [4096, 8], P('dp'), may hold values from 0 to 127, all different within a row; in each aligned block of 128 rows (0 to 127, 128 to 255, ...) at most 16 rows name the same one
- gate_weight: bfloat16 [16, 6144, 2048], P('expert', 'dp'), may hold values from -0.125 to 0.125
- up_weight: bfloat16 [16, 6144, 2048], P('expert', 'dp'), may hold values from -0.125 to 0.125
- down_weight: bfloat16 [16, 6144, 2048], P('expert', 'dp'), may hold values from -0.21875 to 0.21875
- grad_output: bfloat16 [4096, 2048], P('dp', 'expert'), may hold values from -1.75 to 1.75
Outputs:
- mixed: bfloat16 [4096, 2048], P('dp', 'expert')
- grad_tokens: bfloat16 [4096, 2048], P('dp', 'expert')
- grad_route: float32 [4096, 8], P(('dp', 'expert'))
- grad_gate: bfloat16 [16, 6144, 2048], P('expert', 'dp')
- grad_up: bfloat16 [16, 6144, 2048], P('expert', 'dp')
- grad_down: bfloat16 [16, 6144, 2048], P('expert', 'dp')
Inputs may be any that keep to these rules, and one draw needn't show every extreme that they name: `expert_ids`: each token names 8 different experts; among the 128 tokens of one device's aligned block no expert is named more than 16 times, a bound that some block reaches.
All inputs are finite; a program needn't handle non-finite values.
Results may differ from a plain program's by a relative error of at most 0.015.
Values may be sent and summed in bfloat16 or wider, within the bound.
No kernel may reach another device: no remote copies, remote signals or barrier semaphores. Data moves between devices by JAX's collectives and lax.ppermute only.
A program may use at most 64 MiB of HBM per device.

v0:
```python
import jax
import jax.numpy as jnp
from jax import lax
from jax.sharding import PartitionSpec as P

PIECES = 4


def contract_last(left_side, right_side):
    return lax.dot_general(
        left_side, right_side, (((1,), (1,)), ((), ())), preferred_element_type=jnp.float32
    )


def contract_first(left_side, right_side):
    return lax.dot_general(
        left_side, right_side, (((0,), (0,)), ((), ())), preferred_element_type=jnp.float32
    )


def silu_parts(gate_act):
    sigmoid_val = jax.nn.sigmoid(gate_act)
    return (gate_act * sigmoid_val, sigmoid_val * (1.0 + gate_act * (1.0 - sigmoid_val)))


def expert_forward(slot_rows, slot_scale, gate_piece, up_piece, down_piece):
    gate_act = contract_last(slot_rows, gate_piece)
    up_act = contract_last(slot_rows, up_piece)
    active, silu_slope = silu_parts(gate_act)
    hidden = (active * up_act).astype(jnp.bfloat16)
    partial_out = jnp.dot(hidden, down_piece, preferred_element_type=jnp.float32)
    scaled = (slot_scale.astype(jnp.float32)[:, None] * partial_out).astype(jnp.bfloat16)
    return (scaled, gate_act, up_act, hidden)


def on_device(tokens, route_weight, expert_ids, gate_weight, up_weight, down_weight, grad_output):
    groups = lax.axis_size("expert")
    group_index = lax.axis_index("expert")
    data_size = lax.axis_size("dp")
    exp_local = data_size // PIECES
    tok_local, topk_count = expert_ids.shape
    capacity = min(tok_local, 2 * tok_local * topk_count // (exp_local * groups))
    full_tokens, full_grad = (
        lax.all_gather(tokens, "expert", axis=1, tiled=True),
        lax.all_gather(grad_output, "expert", axis=1, tiled=True),
    )
    feature_width = full_tokens.shape[1]
    gate_piece = gate_weight[0]
    up_piece = up_weight[0]
    down_piece = down_weight[0]
    flat_ids = expert_ids.reshape(-1)
    row_count = flat_ids.shape[0]
    owned_rows = flat_ids // exp_local == group_index
    local_ids = flat_ids % exp_local
    chosen = (
        (local_ids[:, None] == jnp.arange(exp_local, dtype=jnp.int32)[None, :])
        & owned_rows[:, None]
    ).astype(jnp.int32)
    slot_ranks = jnp.sum(chosen * (jnp.cumsum(chosen, axis=0) - 1), axis=1)
    slot_count = exp_local * capacity
    slot_pos = jnp.where(owned_rows, local_ids * capacity + slot_ranks, slot_count)
    row_index = jnp.arange(row_count, dtype=jnp.int32)
    row_of = jnp.zeros((slot_count,), jnp.int32).at[slot_pos].set(row_index, mode="drop")
    slot_live = (
        jnp.zeros((slot_count,), jnp.int32).at[slot_pos].set(jnp.ones_like(row_index), mode="drop")
    )
    token_of = row_of // topk_count
    keep_mask = slot_live.astype(tokens.dtype)[:, None]
    slot_weight = route_weight.reshape(-1)[row_of] * slot_live.astype(route_weight.dtype)

    def spread(values):
        trailing = values.shape[1:]
        grouped = values.reshape((exp_local, 1, capacity) + trailing)
        return jnp.broadcast_to(grouped, (exp_local, PIECES, capacity) + trailing).reshape(
            (data_size, capacity) + trailing
        )

    send_rows = spread(full_tokens[token_of] * keep_mask)
    send_weight = spread(slot_weight)
    send_grads = spread(full_grad[token_of] * keep_mask)
    recv_grads = None
    recv_scale = None
    recv_rows, recv_weight = (
        lax.all_to_all(send_rows, "dp", split_axis=0, concat_axis=0, tiled=True),
        lax.all_to_all(send_weight, "dp", split_axis=0, concat_axis=0, tiled=True),
    )
    scaled, gate_act, up_act, hidden = expert_forward(
        recv_rows.reshape(-1, feature_width),
        recv_weight.reshape(-1),
        gate_piece,
        up_piece,
        down_piece,
    )
    returned = lax.all_to_all(
        scaled.reshape(data_size, capacity, feature_width),
        "dp",
        split_axis=0,
        concat_axis=0,
        tiled=True,
    )
    slot_rows = recv_rows.reshape(-1, feature_width)
    wide_token = spread(token_of).reshape(-1)
    wide_live = spread(slot_live).reshape(-1)
    wide_row = spread(row_of).reshape(-1)
    token_place = (
        (wide_token[None, :] == jnp.arange(tok_local, dtype=jnp.int32)[:, None])
        & (wide_live[None, :] > 0)
    ).astype(jnp.bfloat16)
    mixed_sum = jnp.dot(
        token_place, returned.reshape(-1, feature_width), preferred_element_type=jnp.float32
    )
    recv_grads, recv_scale = (
        lax.all_to_all(send_grads, "dp", split_axis=0, concat_axis=0, tiled=True),
        lax.all_to_all(send_weight, "dp", split_axis=0, concat_axis=0, tiled=True),
    )
    active, silu_slope = silu_parts(gate_act)
    slot_grads = recv_grads.reshape(-1, feature_width)
    weight_wide = recv_scale.reshape(-1).astype(jnp.float32)[:, None]
    into_hidden = contract_last(slot_grads, down_piece)
    route_terms = jnp.sum(into_hidden * hidden.astype(jnp.float32), axis=1).astype(jnp.bfloat16)
    hidden_grad = weight_wide * into_hidden
    gate_grad = (hidden_grad * up_act * silu_slope).astype(jnp.bfloat16)
    up_grad = (hidden_grad * active).astype(jnp.bfloat16)
    row_grad = (
        jnp.dot(gate_grad, gate_piece, preferred_element_type=jnp.float32)
        + jnp.dot(up_grad, up_piece, preferred_element_type=jnp.float32)
    ).astype(jnp.bfloat16)
    scaled_grad = (weight_wide * slot_grads.astype(jnp.float32)).astype(jnp.bfloat16)
    grad_gate = contract_first(gate_grad, slot_rows).astype(jnp.bfloat16)[None]
    grad_up = contract_first(up_grad, slot_rows).astype(jnp.bfloat16)[None]
    grad_down = contract_first(hidden, scaled_grad).astype(jnp.bfloat16)[None]
    back_rows, back_terms = (
        lax.all_to_all(
            row_grad.reshape(data_size, capacity, feature_width),
            "dp",
            split_axis=0,
            concat_axis=0,
            tiled=True,
        ),
        lax.all_to_all(
            route_terms.reshape(data_size, capacity), "dp", split_axis=0, concat_axis=0, tiled=True
        ),
    )
    token_sum = jnp.dot(
        token_place, back_rows.reshape(-1, feature_width), preferred_element_type=jnp.float32
    )
    row_place = (
        (wide_row[None, :] == jnp.arange(row_count, dtype=jnp.int32)[:, None])
        & (wide_live[None, :] > 0)
    ).astype(jnp.bfloat16)
    route_sum = jnp.dot(
        row_place, back_terms.reshape(-1), preferred_element_type=jnp.float32
    ).reshape(tok_local, topk_count)
    mixed_part, token_part, route_part = (
        lax.psum_scatter(mixed_sum, "expert", scatter_dimension=1, tiled=True),
        lax.psum_scatter(token_sum, "expert", scatter_dimension=1, tiled=True),
        lax.psum_scatter(route_sum, "expert", scatter_dimension=0, tiled=True),
    )
    return (
        mixed_part.astype(jnp.bfloat16),
        token_part.astype(jnp.bfloat16),
        route_part,
        grad_gate,
        grad_up,
        grad_down,
    )


def solution(mesh):
    return jax.shard_map(
        on_device,
        mesh=mesh,
        in_specs=(
            P("dp", "expert"),
            P("dp", None),
            P("dp", None),
            P("expert", "dp", None),
            P("expert", "dp", None),
            P("expert", "dp", None),
            P("dp", "expert"),
        ),
        out_specs=(
            P("dp", "expert"),
            P("dp", "expert"),
            P(("dp", "expert"), None),
            P("expert", "dp", None),
            P("expert", "dp", None),
            P("expert", "dp", None),
        ),
        check_vma=False,
    )
```

profile of v0, /device:TPU:2, one launch (start us, length us, event | category | flops | bytes accessed | tf_op | source)
XLA Modules:
  0.0 366.5 jit_solution(7416273939957925832)
XLA Ops:
  9.3 2.3 reduce-window.6
  12.2 4.3 %scatter_custom_fusion.1 = s32[128]{0:T(128)S(1)} fusion(s32[1024]{0:T(1024)S(1)} %bitcast.84, s32[1024]{0:T(1024)S(1)} %ne.90, s32[]{:T(128)} %constant.53.clone.1), kind=kCustom, calls=%fused_computation.95 | custom fusion | bytes 516 | tf_op jit(solution)/shard_map/scatter | solution.py:65
  16.5 4.3 %scatter_custom_fusion = s32[128]{0:T(128)S(1)} fusion(s32[1024]{0:T(1024)S(1)} %bitcast.85, s32[1024]{0:T(1024)S(1)} %iota.26, s32[]{:T(128)} %constant.53.clone.1), kind=kCustom, calls=%fused_computation.97 | custom fusion | bytes 516 | tf_op jit(solution)/shard_map/scatter | solution.py:63
  22.9 9.4 %all-to-all-start = ((bf16[32,1,16]{2,1,0:T(2,128)(2,1)}), bf16[32,1,16]{2,1,0:T(2,128)(2,1)S(1)}, u32[]{:S(2)}, u32[]{:S(2)}) async-start(bf16[32,1,16]{2,1,0:T(2,128)(2,1)} %copy.26), calls=%async_computation | async-start | bytes 32768 | tf_op jit(solution)/shard_map/all_to_all | solution.py:85
  32.4 37.0 %all_gather.6 = bf16[128,2048]{1,0:T(8,128)(2,1)S(1)} all-gather(bf16[128,128]{1,0:T(8,128)(2,1)} %param.7), channel_id=1, replica_groups=mesh['dp'=32,'expert'=16] {'expert'}, dimensions={1}, use_global_device_ids=true | all-gather | bytes 557056 | tf_op jit(solution)/shard_map/all_gather | solution.py:44
  69.4 29.3 %all_gather.7 = bf16[128,2048]{1,0:T(8,128)(2,1)S(1)} all-gather(bf16[128,128]{1,0:T(8,128)(2,1)} %param.13), channel_id=1, replica_groups=mesh['dp'=32,'expert'=16] {'expert'}, dimensions={1}, use_global_device_ids=true | all-gather | bytes 557056 | tf_op jit(solution)/shard_map/all_gather | solution.py:45
  101.0 32.6 %all_to_all.36 = bf16[32,16,2048]{2,1,0:T(8,128)(2,1)S(1)} all-to-all(bf16[32,16,2048]{2,1,0:T(8,128)(2,1)S(1)} %bitcast.76), channel_id=1, replica_groups=mesh['dp'=32,'expert'=16] {'dp'}, dimensions={0} | all-to-all | bytes 4194304 | tf_op jit(solution)/shard_map/all_to_all | solution.py:84
  135.2 7.0 %all-to-all-start.3 = ((bf16[32,16,2048]{2,1,0:T(8,128)(2,1)}), bf16[32,16,2048]{2,1,0:T(8,128)(2,1)}, u32[]{:S(2)}, u32[]{:S(2)}) async-start(bf16[32,16,2048]{2,1,0:T(8,128)(2,1)} %bitcast.75), calls=%async_computation.4 | async-start | bytes 4194304 | tf_op jit(solution)/shard_map/all_to_all | solution.py:113
  142.3 2.8 fusion.12
  146.7 21.4 %all-to-all-done.3 = bf16[32,16,2048]{2,1,0:T(8,128)(2,1)} async-done(((bf16[32,16,2048]{2,1,0:T(8,128)(2,1)}), bf16[32,16,2048]{2,1,0:T(8,128)(2,1)}, u32[]{:S(2)}, u32[]{:S(2)}) %all-to-all-start.3) | async-done | bytes 2097184 | tf_op jit(solution)/shard_map/all_to_all | solution.py:113
  168.1 2.7 multiply_reduce_fusion
  171.5 2.0 multiply_convert_fusion.1
  173.6 7.7 %all-to-all-start.2 = ((bf16[32,16,2048]{2,1,0:T(8,128)(2,1)}), bf16[32,16,2048]{2,1,0:T(8,128)(2,1)}, u32[]{:S(2)}, u32[]{:S(2)}) async-start(bf16[32,16,2048]{2,1,0:T(8,128)(2,1)} %bitcast.79), calls=%async_computation.2 | async-start | bytes 4194304 | tf_op jit(solution)/shard_map/all_to_all | solution.py:94
  183.6 2.1 add_convert_fusion
  185.7 21.5 %all-to-all-done.2 = bf16[32,16,2048]{2,1,0:T(8,128)(2,1)} async-done(((bf16[32,16,2048]{2,1,0:T(8,128)(2,1)}), bf16[32,16,2048]{2,1,0:T(8,128)(2,1)}, u32[]{:S(2)}, u32[]{:S(2)}) %all-to-all-start.2) | async-done | bytes 2097184 | tf_op jit(solution)/shard_map/all_to_all | solution.py:94
  207.2 7.7 %all-to-all-start.4 = ((bf16[32,16,2048]{2,1,0:T(8,128)(2,1)}), bf16[32,16,2048]{2,1,0:T(8,128)(2,1)}, u32[]{:S(2)}, u32[]{:S(2)}) async-start(bf16[32,16,2048]{2,1,0:T(8,128)(2,1)} %bitcast.74), calls=%async_computation.5 | async-start | bytes 4194304 | tf_op jit(solution)/shard_map/all_to_all | solution.py:133
  215.0 3.1 fusion.22
  218.3 22.6 %all-to-all-done.4 = bf16[32,16,2048]{2,1,0:T(8,128)(2,1)} async-done(((bf16[32,16,2048]{2,1,0:T(8,128)(2,1)}), bf16[32,16,2048]{2,1,0:T(8,128)(2,1)}, u32[]{:S(2)}, u32[]{:S(2)}) %all-to-all-start.4) | async-done | bytes 2097184 | tf_op jit(solution)/shard_map/all_to_all | solution.py:133
  240.9 3.0 fusion.20
  246.8 6.8 %all-to-all-start.5 = ((bf16[32,1,16]{2,1,0:T(2,128)(2,1)}), bf16[32,1,16]{2,1,0:T(2,128)(2,1)S(1)}, u32[]{:S(2)}, u32[]{:S(2)}) async-start(bf16[32,1,16]{2,1,0:T(2,128)(2,1)} %convert_element_type.95), calls=%async_computation.7 | async-start | bytes 32768 | tf_op jit(solution)/shard_map/all_to_all | solution.py:140
  255.1 3.2 fusion.2
  259.9 2.5 fusion.4
  262.4 54.3 %all-reduce = f32[128,8]{1,0:T(8,128)S(1)} all-reduce(f32[128,8]{1,0:T(8,128)S(1)} %bitcast.80), channel_id=4, replica_groups=mesh['dp'=32,'expert'=16] {'expert'}, use_global_device_ids=true, to_apply=%region_8.9.clone | all-reduce | flops 1024 | bytes 8192
  318.7 39.4 %reduce-scatter.5.cloned.1.call-done = f32[128,128]{1,0:T(8,128)} async-done(((f32[128,2048]{1,0:T(8,128)}), f32[128,128]{1,0:T(8,128)}) %reduce-scatter.5.cloned.1.call-update) | async-done | bytes 65552 | tf_op jit(solution)/shard_map/reduce_scatter | solution.py:156
  (74 shorter events, 22.5 us)
Async XLA Ops:
  7.2 161.0 %copy-start = (bf16[1,192,2048]{2,1,0:T(8,128)(2,1)S(1)}, bf16[1,192,2048]{2,1,0:T(8,128)(2,1)}, u32[]{:S(2)}) copy-start(bf16[1,192,2048]{2,1,0:T(8,128)(2,1)} %param.12) | copy-start | bytes 2359300
  22.9 77.9 %all-to-all-start = ((bf16[32,1,16]{2,1,0:T(2,128)(2,1)}), bf16[32,1,16]{2,1,0:T(2,128)(2,1)S(1)}, u32[]{:S(2)}, u32[]{:S(2)}) async-start(bf16[32,1,16]{2,1,0:T(2,128)(2,1)} %copy.26), calls=%async_computation | async-start | bytes 32768 | tf_op jit(solution)/shard_map/all_to_all | solution.py:85
  135.2 33.0 %all-to-all-start.3 = ((bf16[32,16,2048]{2,1,0:T(8,128)(2,1)}), bf16[32,16,2048]{2,1,0:T(8,128)(2,1)}, u32[]{:S(2)}, u32[]{:S(2)}) async-start(bf16[32,16,2048]{2,1,0:T(8,128)(2,1)} %bitcast.75), calls=%async_computation.4 | async-start | bytes 4194304 | tf_op jit(solution)/shard_map/all_to_all | solution.py:113
  142.3 2.8 copy-start.1
  170.9 0.7 copy-start.3
  173.6 33.6 %all-to-all-start.2 = ((bf16[32,16,2048]{2,1,0:T(8,128)(2,1)}), bf16[32,16,2048]{2,1,0:T(8,128)(2,1)}, u32[]{:S(2)}, u32[]{:S(2)}) async-start(bf16[32,16,2048]{2,1,0:T(8,128)(2,1)} %bitcast.79), calls=%async_computation.2 | async-start | bytes 4194304 | tf_op jit(solution)/shard_map/all_to_all | solution.py:94
  181.7 2.0 copy-start.2
  207.2 33.6 %all-to-all-start.4 = ((bf16[32,16,2048]{2,1,0:T(8,128)(2,1)}), bf16[32,16,2048]{2,1,0:T(8,128)(2,1)}, u32[]{:S(2)}, u32[]{:S(2)}) async-start(bf16[32,16,2048]{2,1,0:T(8,128)(2,1)} %bitcast.74), calls=%async_computation.5 | async-start | bytes 4194304 | tf_op jit(solution)/shard_map/all_to_all | solution.py:133
  214.9 102.4 %reduce-scatter.3.cloned.1.call-start = ((), (), s32[]{:S(2)}) async-start(), calls=%async_computation.8 | async-start | bytes 1114112 | tf_op jit(solution)/shard_map/reduce_scatter | solution.py:155
  218.1 140.1 %reduce-scatter.5.cloned.1.call-start = ((), (), s32[]{:S(2)}) async-start(), calls=%async_computation.9 | async-start | bytes 1114112 | tf_op jit(solution)/shard_map/reduce_scatter | solution.py:156
  246.8 13.0 %all-to-all-start.5 = ((bf16[32,1,16]{2,1,0:T(2,128)(2,1)}), bf16[32,1,16]{2,1,0:T(2,128)(2,1)S(1)}, u32[]{:S(2)}, u32[]{:S(2)}) async-start(bf16[32,1,16]{2,1,0:T(2,128)(2,1)} %convert_element_type.95), calls=%async_computation.7 | async-start | bytes 32768 | tf_op jit(solution)/shard_map/all_to_all | solution.py:140
  253.6 1.5 copy-start.4
Sparse Core Ops, SparseCore 0:
  218.5 67.8 reduce-scatter.2
  289.3 68.8 reduce-scatter.4
where the time goes:
time: 367 us; the launch traced here: 366 us
  blocking collectives  153 us (42%)
  waiting for transfers between devices  105 us (29%)
  starting transfers between devices  38.9 us (11%)
  matrix products  27.9 us (8%)
  local copies, waits for them, and re-layouts  20.7 us (6%)
  between operations  15 us (4%)
  other arithmetic  5.84 us (2%)
    unnamed x1, blocking collectives  54.3 us
    reduce_scatter x1, waiting for transfers between devices, on_device(): lax.psum_scatter(token_sum, 'expert', scatter_dimension=1, tiled=True)  39.4 us
    all_gather x1, blocking collectives, on_device(): lax.all_gather(tokens, 'expert', axis=1, tiled=True)  37 us
    all_to_all x1, blocking collectives, on_device(): lax.all_to_all(send_rows, 'dp', split_axis=0, concat_axis=0, tiled=True)  32.6 us
    all_gather x1, blocking collectives, on_device(): lax.all_gather(grad_output, 'expert', axis=1, tiled=True)  29.3 us
    all_to_all x1, waiting for transfers between devices, on_device(): lax.all_to_all(row_grad.reshape(data_size, capacity, feature_width), 'dp'...  22.6 us
    all_to_all x1, waiting for transfers between devices, on_device(): lax.all_to_all(scaled.reshape(data_size, capacity, feature_width), 'dp',...  21.5 us
    all_to_all x1, waiting for transfers between devices, on_device(): lax.all_to_all(send_grads, 'dp', split_axis=0, concat_axis=0, tiled=True)  21.4 us
  transfers between devices with their start and end apart: 7, of which 5 were waited for; matrix products, arithmetic and copies ran while one was open for 8% of the time, Pallas kernels for 0%

commit v1 on v0

--- a/solution.py
+++ b/solution.py
@@ -4,6 +4,34 @@
 from jax.sharding import PartitionSpec as P
 
 PIECES = 4
+
+
+def wrap_tiles(own_rows, chip_axis, axis_k):
+    kept_arr, val2, next_value = (
+        jax.lax.axis_size(chip_axis),
+        jax.lax.axis_index(chip_axis),
+        own_rows.shape[axis_k],
+    )
+    runs = [no * kept_arr if it == axis_k else no for it, no in enumerate(own_rows.shape)]
+    piece_next = lax.dynamic_update_slice_in_dim(
+        jnp.zeros(runs, own_rows.dtype), own_rows, val2 * next_value, axis=axis_k
+    )
+    heard = t1 = own_rows
+    for hop_no in range(1, kept_arr // 2 + 1):
+        heard = jax.lax.ppermute(
+            heard, chip_axis, list(map(lambda it: (it, (it + 1) % kept_arr), range(kept_arr)))
+        )
+        piece_next = lax.dynamic_update_slice_in_dim(
+            piece_next, heard, (val2 - hop_no) % kept_arr * next_value, axis=axis_k
+        )
+        if 2 * hop_no < kept_arr:
+            t1 = jax.lax.ppermute(
+                t1, chip_axis, list(map(lambda it: (it, (it - 1) % kept_arr), range(kept_arr)))
+            )
+            piece_next = lax.dynamic_update_slice_in_dim(
+                piece_next, t1, (val2 + hop_no) % kept_arr * next_value, axis=axis_k
+            )
+    return piece_next
 
 
 def contract_last(left_side, right_side):
@@ -42,7 +70,7 @@
     capacity = min(tok_local, 2 * tok_local * topk_count // (exp_local * groups))
     full_tokens, full_grad = (
         lax.all_gather(tokens, "expert", axis=1, tiled=True),
-        lax.all_gather(grad_output, "expert", axis=1, tiled=True),
+        wrap_tiles(grad_output, "expert", 1),
     )
     feature_width = full_tokens.shape[1]
     gate_piece = gate_weight[0]

time: 367 us -> 397 us (1.082)
  starting transfers between devices: 38.9 us -> 91.3 us
  blocking collectives: 153 us -> 118 us
  waiting for transfers between devices: 105 us -> 116 us
    ppermute x0 -> x15, starting transfers between devices: none -> 54.5 us  [the longest x7 36.3 us: wrap_tiles(): jax.lax.ppermute(t1, chip_axis, list(map(lambda it: (it, (it - 1) % kept_...]
    all_gather x1 -> x0, blocking collectives: 29.3 us -> none  [on_device(): lax.all_gather(grad_output, 'expert', axis=1, tiled=True)]
    ppermute x0 -> x15, waiting for transfers between devices: none -> 10.1 us  [the longest x8 10.1 us: wrap_tiles(): jax.lax.ppermute(heard, chip_axis, list(map(lambda it: (it, (it + 1) % ke...]
    all_gather x1, blocking collectives: 37 us -> 32.4 us  [on_device(): lax.all_gather(tokens, 'expert', axis=1, tiled=True)]
  transfers between devices with their start and end apart: 7 -> 22, of which waited for: 5 -> 7; matrix products, arithmetic and copies ran while one was open for 8% -> 12% of each run, Pallas kernels for 0% -> 0%
where the time goes in v1:
time: 397 us; the launch traced here: 396 us
  blocking collectives  118 us (30%)
  waiting for transfers between devices  116 us (29%)
  starting transfers between devices  91.3 us (23%)
  matrix products  27.9 us (7%)
  local copies, waits for them, and re-layouts  20.9 us (5%)
  between operations  15.6 us (4%)
  other arithmetic  5.84 us (1%)
    unnamed x1, blocking collectives  52.7 us
    reduce_scatter x1, waiting for transfers between devices, on_device(): lax.psum_scatter(token_sum, 'expert', scatter_dimension=1, tiled=True)  40.3 us
    ppermute x7, starting transfers between devices, wrap_tiles(): jax.lax.ppermute(t1, chip_axis, list(map(lambda it: (it, (it - 1) % kept_...  36.3 us
    all_to_all x1, blocking collectives, on_device(): lax.all_to_all(send_rows, 'dp', split_axis=0, concat_axis=0, tiled=True)  32.6 us
    all_gather x1, blocking collectives, on_device(): lax.all_gather(tokens, 'expert', axis=1, tiled=True)  32.4 us
    all_to_all x1, waiting for transfers between devices, on_device(): lax.all_to_all(row_grad.reshape(data_size, capacity, feature_width), 'dp'...  22.8 us
    all_to_all x1, waiting for transfers between devices, on_device(): lax.all_to_all(scaled.reshape(data_size, capacity, feature_width), 'dp',...  21.6 us
    all_to_all x1, waiting for transfers between devices, on_device(): lax.all_to_all(send_grads, 'dp', split_axis=0, concat_axis=0, tiled=True)  21.4 us
  transfers between devices with their start and end apart: 22, of which 7 were waited for; matrix products, arithmetic and copies ran while one was open for 12% of the time, Pallas kernels for 0%

profile of v1, /device:TPU:2, one launch (start us, length us, event | category | flops | bytes accessed | tf_op | source)
XLA Modules:
  0.0 395.6 jit_solution(13964038984249857254)
XLA Ops:
  7.2 11.5 %collective-permute-start.1 = (bf16[128,128]{1,0:T(8,128)(2,1)}, bf16[128,128]{1,0:T(8,128)(2,1)S(1)}, u32[]{:S(2)}, u32[]{:S(2)}) collective-permute-start(bf16[128,128]{1,0:T(8,128)(2,1)} %param.13), channel_id=1, source_target_pairs={{0,15},{1,0},{2,1},{3,2},{4,3},{5,4},{6,5},{7,6},{8,7},{9,8},{10,9... | collective-permute-start | bytes 98312 | tf_op jit(solution)/shard_map/ppermute | solution.py:28
  25.6 4.3 %scatter_custom_fusion.1 = s32[128]{0:T(128)S(1)} fusion(s32[1024]{0:T(1024)S(1)} %bitcast.84, s32[1024]{0:T(1024)S(1)} %ne.152, s32[]{:T(128)} %constant.136.clone.1), kind=kCustom, calls=%fused_computation.111 | custom fusion | bytes 516 | tf_op jit(solution)/shard_map/scatter | solution.py:93
  29.9 4.3 %scatter_custom_fusion = s32[128]{0:T(128)S(1)} fusion(s32[1024]{0:T(1024)S(1)} %bitcast.85, s32[1024]{0:T(1024)S(1)} %iota.26, s32[]{:T(128)} %constant.136.clone.1), kind=kCustom, calls=%fused_computation.113 | custom fusion | bytes 516 | tf_op jit(solution)/shard_map/scatter | solution.py:91
  36.3 7.6 %all-to-all-start = ((bf16[32,1,16]{2,1,0:T(2,128)(2,1)}), bf16[32,1,16]{2,1,0:T(2,128)(2,1)S(1)}, u32[]{:S(2)}, u32[]{:S(2)}) async-start(bf16[32,1,16]{2,1,0:T(2,128)(2,1)} %copy.26), calls=%async_computation | async-start | bytes 32768 | tf_op jit(solution)/shard_map/all_to_all | solution.py:113
  43.9 32.4 %all_gather.3 = bf16[128,2048]{1,0:T(8,128)(2,1)S(1)} all-gather(bf16[128,128]{1,0:T(8,128)(2,1)} %param.7), channel_id=1, replica_groups=mesh['dp'=32,'expert'=16] {'expert'}, dimensions={1}, use_global_device_ids=true | all-gather | bytes 557056 | tf_op jit(solution)/shard_map/all_gather | solution.py:72
  79.7 3.9 collective-permute-start.2
  83.7 3.1 collective-permute-start.5
  89.6 4.3 %collective-permute-start.7 = (bf16[128,128]{1,0:T(8,128)(2,1)S(1)}, bf16[128,128]{1,0:T(8,128)(2,1)S(1)}, u32[]{:S(2)}, u32[]{:S(2)}) collective-permute-start(bf16[128,128]{1,0:T(8,128)(2,1)S(1)} %collective-permute-done.5), channel_id=1, source_target_pairs={{0,15},{1,0},{2,1},{3,2},{4,3},{5,4},{6,5},{7,6},{8,7},{9,8},{10,9... | collective-permute-start | bytes 98312 | tf_op jit(solution)/shard_map/ppermute | solution.py:28
  96.0 5.1 %collective-permute-start.9 = (bf16[128,128]{1,0:T(8,128)(2,1)S(1)}, bf16[128,128]{1,0:T(8,128)(2,1)S(1)}, u32[]{:S(2)}, u32[]{:S(2)}) collective-permute-start(bf16[128,128]{1,0:T(8,128)(2,1)S(1)} %collective-permute-done.7), channel_id=1, source_target_pairs={{0,15},{1,0},{2,1},{3,2},{4,3},{5,4},{6,5},{7,6},{8,7},{9,8},{10,9... | collective-permute-start | bytes 98312 | tf_op jit(solution)/shard_map/ppermute | solution.py:28
  103.1 5.1 %collective-permute-start.11 = (bf16[128,128]{1,0:T(8,128)(2,1)S(1)}, bf16[128,128]{1,0:T(8,128)(2,1)S(1)}, u32[]{:S(2)}, u32[]{:S(2)}) collective-permute-start(bf16[128,128]{1,0:T(8,128)(2,1)S(1)} %collective-permute-done.9), channel_id=1, source_target_pairs={{0,15},{1,0},{2,1},{3,2},{4,3},{5,4},{6,5},{7,6},{8,7},{9,8},{10,9... | collective-permute-start | bytes 98312 | tf_op jit(solution)/shard_map/ppermute | solution.py:28
  110.2 5.1 %collective-permute-start.13 = (bf16[128,128]{1,0:T(8,128)(2,1)S(1)}, bf16[128,128]{1,0:T(8,128)(2,1)S(1)}, u32[]{:S(2)}, u32[]{:S(2)}) collective-permute-start(bf16[128,128]{1,0:T(8,128)(2,1)S(1)} %collective-permute-done.11), channel_id=1, source_target_pairs={{0,15},{1,0},{2,1},{3,2},{4,3},{5,4},{6,5},{7,6},{8,7},{9,8},{10,9... | collective-permute-start | bytes 98312 | tf_op jit(solution)/shard_map/ppermute | solution.py:28
  117.4 5.0 %collective-permute-done.12 = bf16[128,128]{1,0:T(8,128)(2,1)S(1)} collective-permute-done((bf16[128,128]{1,0:T(8,128)(2,1)S(1)}, bf16[128,128]{1,0:T(8,128)(2,1)S(1)}, u32[]{:S(2)}, u32[]{:S(2)}) %collective-permute-start.12) | collective-permute-done | bytes 32800 | tf_op jit(solution)/shard_map/ppermute | solution.py:21
  124.4 5.0 %collective-permute-done.14 = bf16[128,128]{1,0:T(8,128)(2,1)S(1)} collective-permute-done((bf16[128,128]{1,0:T(8,128)(2,1)S(1)}, bf16[128,128]{1,0:T(8,128)(2,1)S(1)}, u32[]{:S(2)}, u32[]{:S(2)}) %collective-permute-start.14) | collective-permute-done | bytes 32800 | tf_op jit(solution)/shard_map/ppermute | solution.py:21
  130.8 32.6 %all_to_all.36 = bf16[32,16,2048]{2,1,0:T(8,128)(2,1)S(1)} all-to-all(bf16[32,16,2048]{2,1,0:T(8,128)(2,1)S(1)} %bitcast.76), channel_id=1, replica_groups=mesh['dp'=32,'expert'=16] {'dp'}, dimensions={0} | all-to-all | bytes 4194304 | tf_op jit(solution)/shard_map/all_to_all | solution.py:112
  164.9 7.0 %all-to-all-start.3 = ((bf16[32,16,2048]{2,1,0:T(8,128)(2,1)}), bf16[32,16,2048]{2,1,0:T(8,128)(2,1)}, u32[]{:S(2)}, u32[]{:S(2)}) async-start(bf16[32,16,2048]{2,1,0:T(8,128)(2,1)} %bitcast.75), calls=%async_computation.4 | async-start | bytes 4194304 | tf_op jit(solution)/shard_map/all_to_all | solution.py:141
  176.5 21.4 %all-to-all-done.3 = bf16[32,16,2048]{2,1,0:T(8,128)(2,1)} async-done(((bf16[32,16,2048]{2,1,0:T(8,128)(2,1)}), bf16[32,16,2048]{2,1,0:T(8,128)(2,1)}, u32[]{:S(2)}, u32[]{:S(2)}) %all-to-all-start.3) | async-done | bytes 2097184 | tf_op jit(solution)/shard_map/all_to_all | solution.py:141
  203.4 7.7 %all-to-all-start.2 = ((bf16[32,16,2048]{2,1,0:T(8,128)(2,1)}), bf16[32,16,2048]{2,1,0:T(8,128)(2,1)}, u32[]{:S(2)}, u32[]{:S(2)}) async-start(bf16[32,16,2048]{2,1,0:T(8,128)(2,1)} %bitcast.79), calls=%async_computation.2 | async-start | bytes 4194304 | tf_op jit(solution)/shard_map/all_to_all | solution.py:122
  215.5 21.6 %all-to-all-done.2 = bf16[32,16,2048]{2,1,0:T(8,128)(2,1)} async-done(((bf16[32,16,2048]{2,1,0:T(8,128)(2,1)}), bf16[32,16,2048]{2,1,0:T(8,128)(2,1)}, u32[]{:S(2)}, u32[]{:S(2)}) %all-to-all-start.2) | async-done | bytes 2097184 | tf_op jit(solution)/shard_map/all_to_all | solution.py:122
  237.1 7.6 %all-to-all-start.4 = ((bf16[32,16,2048]{2,1,0:T(8,128)(2,1)}), bf16[32,16,2048]{2,1,0:T(8,128)(2,1)}, u32[]{:S(2)}, u32[]{:S(2)}) async-start(bf16[32,16,2048]{2,1,0:T(8,128)(2,1)} %bitcast.74), calls=%async_computation.5 | async-start | bytes 4194304 | tf_op jit(solution)/shard_map/all_to_all | solution.py:161
  247.9 22.8 %all-to-all-done.4 = bf16[32,16,2048]{2,1,0:T(8,128)(2,1)} async-done(((bf16[32,16,2048]{2,1,0:T(8,128)(2,1)}), bf16[32,16,2048]{2,1,0:T(8,128)(2,1)}, u32[]{:S(2)}, u32[]{:S(2)}) %all-to-all-start.4) | async-done | bytes 2097184 | tf_op jit(solution)/shard_map/all_to_all | solution.py:161
  276.5 6.8 %all-to-all-start.5 = ((bf16[32,1,16]{2,1,0:T(2,128)(2,1)}), bf16[32,1,16]{2,1,0:T(2,128)(2,1)S(1)}, u32[]{:S(2)}, u32[]{:S(2)}) async-start(bf16[32,1,16]{2,1,0:T(2,128)(2,1)} %convert_element_type.95), calls=%async_computation.7 | async-start | bytes 32768 | tf_op jit(solution)/shard_map/all_to_all | solution.py:168
  284.9 3.2 fusion.2
  292.2 52.7 %all-reduce = f32[128,8]{1,0:T(8,128)S(1)} all-reduce(f32[128,8]{1,0:T(8,128)S(1)} %bitcast.80), channel_id=4, replica_groups=mesh['dp'=32,'expert'=16] {'expert'}, use_global_device_ids=true, to_apply=%region_8.9.clone | all-reduce | flops 1024 | bytes 8192
  347.0 40.3 %reduce-scatter.5.cloned.1.call-done = f32[128,128]{1,0:T(8,128)} async-done(((f32[128,2048]{1,0:T(8,128)}), f32[128,128]{1,0:T(8,128)}) %reduce-scatter.5.cloned.1.call-update) | async-done | bytes 65552 | tf_op jit(solution)/shard_map/reduce_scatter | solution.py:184
  (122 shorter events, 59.3 us)
Async XLA Ops:
  7.2 190.7 %copy-start = (bf16[1,192,2048]{2,1,0:T(8,128)(2,1)S(1)}, bf16[1,192,2048]{2,1,0:T(8,128)(2,1)}, u32[]{:S(2)}) copy-start(bf16[1,192,2048]{2,1,0:T(8,128)(2,1)} %param.12) | copy-start | bytes 2359300
  7.2 69.2 %copy-start.3 = (bf16[128,128]{1,0:T(8,128)(2,1)S(1)}, bf16[128,128]{1,0:T(8,128)(2,1)}, u32[]{:S(2)}) copy-start(bf16[128,128]{1,0:T(8,128)(2,1)} %param.13) | copy-start | bytes 98308
  7.2 70.6 %collective-permute-start.1 = (bf16[128,128]{1,0:T(8,128)(2,1)}, bf16[128,128]{1,0:T(8,128)(2,1)S(1)}, u32[]{:S(2)}, u32[]{:S(2)}) collective-permute-start(bf16[128,128]{1,0:T(8,128)(2,1)} %param.13), channel_id=1, source_target_pairs={{0,15},{1,0},{2,1},{3,2},{4,3},{5,4},{6,5},{7,6},{8,7},{9,8},{10,9... | collective-permute-start | bytes 98312 | tf_op jit(solution)/shard_map/ppermute | solution.py:28
  18.7 61.0 %collective-permute-start = (bf16[128,128]{1,0:T(8,128)(2,1)}, bf16[128,128]{1,0:T(8,128)(2,1)S(1)}, u32[]{:S(2)}, u32[]{:S(2)}) collective-permute-start(bf16[128,128]{1,0:T(8,128)(2,1)} %param.13), channel_id=1, source_target_pairs={{0,1},{1,2},{2,3},{3,4},{4,5},{5,6},{6,7},{7,8},{8,9},{9,10},{10,1... | collective-permute-start | bytes 98312 | tf_op jit(solution)/shard_map/ppermute | solution.py:21
  36.3 94.2 %all-to-all-start = ((bf16[32,1,16]{2,1,0:T(2,128)(2,1)}), bf16[32,1,16]{2,1,0:T(2,128)(2,1)S(1)}, u32[]{:S(2)}, u32[]{:S(2)}) async-start(bf16[32,1,16]{2,1,0:T(2,128)(2,1)} %copy.26), calls=%async_computation | async-start | bytes 32768 | tf_op jit(solution)/shard_map/all_to_all | solution.py:113
  77.8 5.9 %collective-permute-start.3 = (bf16[128,128]{1,0:T(8,128)(2,1)S(1)}, bf16[128,128]{1,0:T(8,128)(2,1)S(1)}, u32[]{:S(2)}, u32[]{:S(2)}) collective-permute-start(bf16[128,128]{1,0:T(8,128)(2,1)S(1)} %collective-permute-done.1), channel_id=1, source_target_pairs={{0,15},{1,0},{2,1},{3,2},{4,3},{5,4},{6,5},{7,6},{8,7},{9,8},{10,9... | collective-permute-start | bytes 98312 | tf_op jit(solution)/shard_map/ppermute | solution.py:28
  79.7 7.1 %collective-permute-start.2 = (bf16[128,128]{1,0:T(8,128)(2,1)S(1)}, bf16[128,128]{1,0:T(8,128)(2,1)S(1)}, u32[]{:S(2)}, u32[]{:S(2)}) collective-permute-start(bf16[128,128]{1,0:T(8,128)(2,1)S(1)} %collective-permute-done), channel_id=1, source_target_pairs={{0,1},{1,2},{2,3},{3,4},{4,5},{5,6},{6,7},{7,8},{8,9},{9,10},{10,1... | collective-permute-start | bytes 98312 | tf_op jit(solution)/shard_map/ppermute | solution.py:21
  83.7 5.9 %collective-permute-start.5 = (bf16[128,128]{1,0:T(8,128)(2,1)S(1)}, bf16[128,128]{1,0:T(8,128)(2,1)S(1)}, u32[]{:S(2)}, u32[]{:S(2)}) collective-permute-start(bf16[128,128]{1,0:T(8,128)(2,1)S(1)} %collective-permute-done.3), channel_id=1, source_target_pairs={{0,15},{1,0},{2,1},{3,2},{4,3},{5,4},{6,5},{7,6},{8,7},{9,8},{10,9... | collective-permute-start | bytes 98312 | tf_op jit(solution)/shard_map/ppermute | solution.py:28
  86.8 7.1 %collective-permute-start.4 = (bf16[128,128]{1,0:T(8,128)(2,1)S(1)}, bf16[128,128]{1,0:T(8,128)(2,1)S(1)}, u32[]{:S(2)}, u32[]{:S(2)}) collective-permute-start(bf16[128,128]{1,0:T(8,128)(2,1)S(1)} %collective-permute-done.2), channel_id=1, source_target_pairs={{0,1},{1,2},{2,3},{3,4},{4,5},{5,6},{6,7},{7,8},{8,9},{9,10},{10,1... | collective-permute-start | bytes 98312 | tf_op jit(solution)/shard_map/ppermute | solution.py:21
  89.6 6.3 %collective-permute-start.7 = (bf16[128,128]{1,0:T(8,128)(2,1)S(1)}, bf16[128,128]{1,0:T(8,128)(2,1)S(1)}, u32[]{:S(2)}, u32[]{:S(2)}) collective-permute-start(bf16[128,128]{1,0:T(8,128)(2,1)S(1)} %collective-permute-done.5), channel_id=1, source_target_pairs={{0,15},{1,0},{2,1},{3,2},{4,3},{5,4},{6,5},{7,6},{8,7},{9,8},{10,9... | collective-permute-start | bytes 98312 | tf_op jit(solution)/shard_map/ppermute | solution.py:28
  94.0 7.1 %collective-permute-start.6 = (bf16[128,128]{1,0:T(8,128)(2,1)S(1)}, bf16[128,128]{1,0:T(8,128)(2,1)S(1)}, u32[]{:S(2)}, u32[]{:S(2)}) collective-permute-start(bf16[128,128]{1,0:T(8,128)(2,1)S(1)} %collective-permute-done.4), channel_id=1, source_target_pairs={{0,1},{1,2},{2,3},{3,4},{4,5},{5,6},{6,7},{7,8},{8,9},{9,10},{10,1... | collective-permute-start | bytes 98312 | tf_op jit(solution)/shard_map/ppermute | solution.py:21
  96.0 7.1 %collective-permute-start.9 = (bf16[128,128]{1,0:T(8,128)(2,1)S(1)}, bf16[128,128]{1,0:T(8,128)(2,1)S(1)}, u32[]{:S(2)}, u32[]{:S(2)}) collective-permute-start(bf16[128,128]{1,0:T(8,128)(2,1)S(1)} %collective-permute-done.7), channel_id=1, source_target_pairs={{0,15},{1,0},{2,1},{3,2},{4,3},{5,4},{6,5},{7,6},{8,7},{9,8},{10,9... | collective-permute-start | bytes 98312 | tf_op jit(solution)/shard_map/ppermute | solution.py:28
  101.1 7.1 %collective-permute-start.8 = (bf16[128,128]{1,0:T(8,128)(2,1)S(1)}, bf16[128,128]{1,0:T(8,128)(2,1)S(1)}, u32[]{:S(2)}, u32[]{:S(2)}) collective-permute-start(bf16[128,128]{1,0:T(8,128)(2,1)S(1)} %collective-permute-done.6), channel_id=1, source_target_pairs={{0,1},{1,2},{2,3},{3,4},{4,5},{5,6},{6,7},{7,8},{8,9},{9,10},{10,1... | collective-permute-start | bytes 98312 | tf_op jit(solution)/shard_map/ppermute | solution.py:21
  103.1 7.1 %collective-permute-start.11 = (bf16[128,128]{1,0:T(8,128)(2,1)S(1)}, bf16[128,128]{1,0:T(8,128)(2,1)S(1)}, u32[]{:S(2)}, u32[]{:S(2)}) collective-permute-start(bf16[128,128]{1,0:T(8,128)(2,1)S(1)} %collective-permute-done.9), channel_id=1, source_target_pairs={{0,15},{1,0},{2,1},{3,2},{4,3},{5,4},{6,5},{7,6},{8,7},{9,8},{10,9... | collective-permute-start | bytes 98312 | tf_op jit(solution)/shard_map/ppermute | solution.py:28
  108.3 7.1 %collective-permute-start.10 = (bf16[128,128]{1,0:T(8,128)(2,1)S(1)}, bf16[128,128]{1,0:T(8,128)(2,1)S(1)}, u32[]{:S(2)}, u32[]{:S(2)}) collective-permute-start(bf16[128,128]{1,0:T(8,128)(2,1)S(1)} %collective-permute-done.8), channel_id=1, source_target_pairs={{0,1},{1,2},{2,3},{3,4},{4,5},{5,6},{6,7},{7,8},{8,9},{9,10},{10,1... | collective-permute-start | bytes 98312 | tf_op jit(solution)/shard_map/ppermute | solution.py:21
  110.2 14.1 %collective-permute-start.13 = (bf16[128,128]{1,0:T(8,128)(2,1)S(1)}, bf16[128,128]{1,0:T(8,128)(2,1)S(1)}, u32[]{:S(2)}, u32[]{:S(2)}) collective-permute-start(bf16[128,128]{1,0:T(8,128)(2,1)S(1)} %collective-permute-done.11), channel_id=1, source_target_pairs={{0,15},{1,0},{2,1},{3,2},{4,3},{5,4},{6,5},{7,6},{8,7},{9,8},{10,9... | collective-permute-start | bytes 98312 | tf_op jit(solution)/shard_map/ppermute | solution.py:28
  115.4 7.0 %collective-permute-start.12 = (bf16[128,128]{1,0:T(8,128)(2,1)S(1)}, bf16[128,128]{1,0:T(8,128)(2,1)S(1)}, u32[]{:S(2)}, u32[]{:S(2)}) collective-permute-start(bf16[128,128]{1,0:T(8,128)(2,1)S(1)} %collective-permute-done.10), channel_id=1, source_target_pairs={{0,1},{1,2},{2,3},{3,4},{4,5},{5,6},{6,7},{7,8},{8,9},{9,10},{10,1... | collective-permute-start | bytes 98312 | tf_op jit(solution)/shard_map/ppermute | solution.py:21
  122.4 7.0 %collective-permute-start.14 = (bf16[128,128]{1,0:T(8,128)(2,1)S(1)}, bf16[128,128]{1,0:T(8,128)(2,1)S(1)}, u32[]{:S(2)}, u32[]{:S(2)}) collective-permute-start(bf16[128,128]{1,0:T(8,128)(2,1)S(1)} %collective-permute-done.12), channel_id=1, source_target_pairs={{0,1},{1,2},{2,3},{3,4},{4,5},{5,6},{6,7},{7,8},{8,9},{9,10},{10,1... | collective-permute-start | bytes 98312 | tf_op jit(solution)/shard_map/ppermute | solution.py:21
  164.9 33.0 %all-to-all-start.3 = ((bf16[32,16,2048]{2,1,0:T(8,128)(2,1)}), bf16[32,16,2048]{2,1,0:T(8,128)(2,1)}, u32[]{:S(2)}, u32[]{:S(2)}) async-start(bf16[32,16,2048]{2,1,0:T(8,128)(2,1)} %bitcast.75), calls=%async_computation.4 | async-start | bytes 4194304 | tf_op jit(solution)/shard_map/all_to_all | solution.py:141
  203.4 33.7 %all-to-all-start.2 = ((bf16[32,16,2048]{2,1,0:T(8,128)(2,1)}), bf16[32,16,2048]{2,1,0:T(8,128)(2,1)}, u32[]{:S(2)}, u32[]{:S(2)}) async-start(bf16[32,16,2048]{2,1,0:T(8,128)(2,1)} %bitcast.79), calls=%async_computation.2 | async-start | bytes 4194304 | tf_op jit(solution)/shard_map/all_to_all | solution.py:122
  237.1 33.6 %all-to-all-start.4 = ((bf16[32,16,2048]{2,1,0:T(8,128)(2,1)}), bf16[32,16,2048]{2,1,0:T(8,128)(2,1)}, u32[]{:S(2)}, u32[]{:S(2)}) async-start(bf16[32,16,2048]{2,1,0:T(8,128)(2,1)} %bitcast.74), calls=%async_computation.5 | async-start | bytes 4194304 | tf_op jit(solution)/shard_map/all_to_all | solution.py:161
  244.7 100.8 %reduce-scatter.3.cloned.1.call-start = ((), (), s32[]{:S(2)}) async-start(), calls=%async_computation.8 | async-start | bytes 1114112 | tf_op jit(solution)/shard_map/reduce_scatter | solution.py:183
  247.9 139.4 %reduce-scatter.5.cloned.1.call-start = ((), (), s32[]{:S(2)}) async-start(), calls=%async_computation.9 | async-start | bytes 1114112 | tf_op jit(solution)/shard_map/reduce_scatter | solution.py:184
  276.5 13.0 %all-to-all-start.5 = ((bf16[32,1,16]{2,1,0:T(2,128)(2,1)}), bf16[32,1,16]{2,1,0:T(2,128)(2,1)S(1)}, u32[]{:S(2)}, u32[]{:S(2)}) async-start(bf16[32,1,16]{2,1,0:T(2,128)(2,1)} %convert_element_type.95), calls=%async_computation.7 | async-start | bytes 32768 | tf_op jit(solution)/shard_map/all_to_all | solution.py:168
  (4 other events, 6.9 us)
Sparse Core Ops, SparseCore 0:
  248.3 67.0 reduce-scatter.2
  318.2 69.0 reduce-scatter.4
